TPU v7x, 32 devices: a whole 2x2x4 slice. The times are simulated.
32 devices in a mesh: tile: 8 (over y, x, core), mem: 4 (over z).
Axes of the slice: x: 2, y: 2, z: 4, core: 2. Of those that a mesh axis runs over, the one named last changes fastest.
Arguments:
- control: bfloat16 [80, 1, 360, 720], P('mem', None, 'tile'), may hold values from -6 to 6
- perturb: bfloat16 [80, 1, 360, 720], P('mem', None, 'tile'), may hold values from -6 to 6
- lon_taps: bfloat16 [17], replicated, may hold values from 0.026367188 to 0.07910156
- lat_taps: bfloat16 [17], replicated, may hold values from 0.026367188 to 0.07910156
- innov: float32 [8, 8, 256], P('tile'), may hold values from -6 to 6
- inv_var: float32 [8, 8, 256], P('tile'), may hold values from 1 to 8
- cell_index: int32 [8, 8, 256], P('tile'), may hold values from 0 to 32399, as said below
- counts: int32 [8, 8], P('tile'), may hold values from 0 to 256, as said below
Outputs:
- gradient: float32 [80, 1, 360, 720], P('mem', None, 'tile')
Inputs may be any that keep to these rules, and one draw needn't show every extreme that they name: `cell_index`: an observation's cell within its owning tile, level * 45 * 720 + longitude within the tile * 720 + latitude; both ends are taken. `counts`: live slots per pair of tiles; some pair fills all 256 slots in every draw, and some owning tiles receive far more than others.
All inputs are finite; a program needn't handle non-finite values.
Results may differ from a plain program's by a relative error of at most 0.00066.
Values may be sent and summed in bfloat16 or wider, within the bound.
No kernel may reach another device: no remote copies, remote signals or barrier semaphores. Data moves between devices by JAX's collectives and lax.ppermute only.
A program may use at most 64 MiB of HBM per device.

v0:
```python
import math
import jax
import jax.numpy as jnp
from jax import lax
from jax.sharding import PartitionSpec as P


def extended_2(block, sides, width):
    for axis, dim in sides:
        count = lax.axis_size(axis)
        forward = [(i, i + 1) for i in range(count - 1)]
        forward.append((count - 1, 0))
        backward = [(target, source) for source, target in forward]
        low = lax.ppermute(
            lax.slice_in_dim(block, block.shape[dim] - width, None, axis=dim), axis, forward
        )
        high = lax.ppermute(lax.slice_in_dim(block, 0, width, axis=dim), axis, backward)
        block = jnp.concatenate([low, block, high], axis=dim)
    return block


def band_from(offsets, tap_weights):
    radius = tap_weights.shape[0] - 1
    taps = tap_weights.astype(jnp.float32)
    band = jnp.zeros(offsets.shape, jnp.float32)
    for offset in range(radius + 1):
        band = band + jnp.where(offsets == offset, taps[offset], 0.0)
    return band.astype(jnp.bfloat16)


def lon_band(tap_weights, lon_cells):
    radius = tap_weights.shape[0] - 1
    row_ids = lax.broadcasted_iota(jnp.int32, (lon_cells, lon_cells + 2 * radius), 0)
    col_ids = lax.broadcasted_iota(jnp.int32, (lon_cells, lon_cells + 2 * radius), 1)
    return band_from(jnp.abs(col_ids - row_ids - radius), tap_weights)


def lat_block_band(tap_weights, block_cells):
    radius = tap_weights.shape[0] - 1
    row_ids = lax.broadcasted_iota(jnp.int32, (block_cells + 2 * radius, block_cells), 0)
    col_ids = lax.broadcasted_iota(jnp.int32, (block_cells + 2 * radius, block_cells), 1)
    return band_from(jnp.abs(row_ids - radius - col_ids), tap_weights)


def localize(extended, band_lon, band_blocks, radius, block_cells):
    along = jnp.einsum(
        "ij,mljk->mlik", band_lon, extended, preferred_element_type=jnp.float32
    ).astype(jnp.bfloat16)
    members_here, levels, lon_cells, lat_cells = along.shape
    padded = jnp.pad(along, ((0, 0), (0, 0), (0, 0), (radius, radius)))
    block_count = lat_cells // block_cells
    windows = jnp.stack(
        [
            padded[:, :, :, block * block_cells : block * block_cells + block_cells + 2 * radius]
            for block in range(block_count)
        ],
        axis=3,
    )
    result = jnp.einsum("mlibk,kq->mlibq", windows, band_blocks, preferred_element_type=jnp.float32)
    return result.reshape(members_here, levels, lon_cells, lat_cells)


def pick_cells(field_rows, row_index, col_index, block_rows):
    row_count, col_count = field_rows.shape
    field_cols = field_rows.T

    def pick_one_block(indices):
        rows_here, cols_here = indices
        onehot_rows = (
            rows_here[:, None] == jnp.arange(row_count, dtype=jnp.int32)[None, :]
        ).astype(jnp.float32)
        onehot_cols = (
            cols_here[:, None] == jnp.arange(col_count, dtype=jnp.int32)[None, :]
        ).astype(jnp.float32)
        picked = jnp.dot(
            onehot_cols,
            field_cols,
            precision=lax.Precision.HIGHEST,
            preferred_element_type=jnp.float32,
        )
        return jnp.sum(picked * onehot_rows, axis=1)

    values = lax.map(
        pick_one_block, (row_index.reshape(-1, block_rows), col_index.reshape(-1, block_rows))
    )
    return values.reshape(-1)


def spread_cells(misfit, row_index, col_index, row_count, col_count, block_rows):

    def spread_one_block(total, items):
        rows_here, cols_here, values = items
        onehot_rows = (
            rows_here[:, None] == jnp.arange(row_count, dtype=jnp.int32)[None, :]
        ).astype(jnp.float32)
        onehot_cols = (
            cols_here[:, None] == jnp.arange(col_count, dtype=jnp.int32)[None, :]
        ).astype(jnp.float32)
        weighted = onehot_rows * values[:, None]
        return (
            total
            + jnp.dot(
                weighted.T,
                onehot_cols,
                precision=lax.Precision.HIGHEST,
                preferred_element_type=jnp.float32,
            ),
            None,
        )

    start = jnp.zeros((row_count, col_count), jnp.float32)
    items = (
        row_index.reshape(-1, block_rows),
        col_index.reshape(-1, block_rows),
        misfit.reshape(-1, block_rows),
    )
    total, _ = lax.scan(spread_one_block, start, items)
    return total


def local(control, perturb, lon_taps, lat_taps, innov, inv_var, cell_index, counts):
    members_here, levels, lon_cells, lat_cells = control.shape
    radius = lon_taps.shape[0] - 1
    block_cells = 144
    band_lon = lon_band(lon_taps, lon_cells)
    band_blocks = lat_block_band(lat_taps, block_cells)
    extended = extended_2(control, (("tile", 2),), radius)
    smoothed = localize(extended, band_lon, band_blocks, radius, block_cells)
    member_sum = jnp.sum(perturb.astype(jnp.float32) * smoothed, axis=0)
    slot_ids = lax.broadcasted_iota(jnp.int32, innov.shape, 2)
    is_live = slot_ids < counts[:, :, None]
    weights = jnp.where(is_live, inv_var, 0.0)
    received = (
        lax.all_to_all(innov, "tile", split_axis=1, concat_axis=0, tiled=True),
        lax.all_to_all(weights, "tile", split_axis=1, concat_axis=0, tiled=True),
        lax.all_to_all(cell_index, "tile", split_axis=1, concat_axis=0, tiled=True),
    )
    observed = received[0].reshape(-1)
    weight_recv = received[1].reshape(-1)
    cells_hit = received[2].reshape(-1)
    row_index = cells_hit // lat_cells
    col_index = cells_hit % lat_cells
    row_count = levels * lon_cells
    block_rows = math.gcd(observed.shape[0], 1024)
    increment = lax.psum(member_sum, "mem")
    at_cells = pick_cells(increment.reshape(row_count, lat_cells), row_index, col_index, block_rows)
    misfit = weight_recv * (at_cells - observed)
    spread = spread_cells(misfit, row_index, col_index, row_count, lat_cells, block_rows)
    spread = spread.reshape(levels, lon_cells, lat_cells)
    wide_pert = extended_2(perturb, (("tile", 2),), radius)
    wide_spread = extended_2(spread, (("tile", 1),), radius)
    wide_products = (wide_pert.astype(jnp.float32) * wide_spread[None]).astype(jnp.bfloat16)
    return control.astype(jnp.float32) + localize(
        wide_products, band_lon, band_blocks, radius, block_cells
    )


def solution(mesh):
    return jax.shard_map(
        local,
        mesh=mesh,
        in_specs=(
            P("mem", None, "tile", None),
            P("mem", None, "tile", None),
            P(),
            P(),
            P("tile", None, None),
            P("tile", None, None),
            P("tile", None, None),
            P("tile", None),
        ),
        out_specs=P("mem", None, "tile", None),
        check_vma=False,
    )
```

profile of v0, /device:TPU:11, one launch (start us, length us, event | category | flops | bytes accessed | tf_op | source)
XLA Modules:
  0.0 176.9 jit_solution(8008073635435257452)
XLA Ops:
  6.6 1.5 fusion.166
  8.1 1.8 %collective-permute-start.2 = (bf16[20,1,16,720]{3,2,0,1:T(8,128)(2,1)S(1)}, bf16[20,1,16,720]{3,2,0,1:T(8,128)(2,1)}, u32[]{:S(2)}, u32[]{:S(2)}) collective-permute-start(bf16[20,1,16,720]{3,2,0,1:T(8,128)(2,1)S(1)} %get-tuple-element.115), channel_id=1, source_target_pairs={{0,4},{4,8},{8,12},{12,16},{16,20},{20,24},{24,28},{28,0},{1,5},{5... | collective-permute-start | bytes 1382408 | tf_op jit(solution)/shard_map/ppermute | solution.py:14
  9.9 1.3 copy.48
  11.2 4.9 %all-to-all-start = ((s32[1,8,256]{2,0,1:T(1,128)}), s32[1,8,256]{2,0,1:T(1,128)S(1)}, u32[]{:S(2)}, u32[]{:S(2)}) async-start(s32[1,8,256]{2,0,1:T(1,128)} %copy.48), calls=%async_computation | async-start | bytes 16384 | tf_op jit(solution)/shard_map/all_to_all | solution.py:136
  16.1 2.2 %fusion.167 = (bf16[20,1,16,720]{3,2,0,1:T(8,128)(2,1)}, bf16[20,1,16,720]{3,2,0,1:T(8,128)(2,1)S(1)}) fusion(bf16[20,1,45,720]{3,2,0,1:T(8,128)(2,1)} %bitcast.147), kind=kLoop, calls=%fused_computation.200 | loop fusion | bytes 1843200 | tf_op jit(solution)/shard_map/slice | solution.py:15
  18.3 1.5 collective-permute-start
  23.2 4.4 %all-to-all-start.1 = ((f32[1,8,256]{2,0,1:T(1,128)}), f32[1,8,256]{2,0,1:T(1,128)S(1)}, u32[]{:S(2)}, u32[]{:S(2)}) async-start(f32[1,8,256]{2,0,1:T(1,128)} %compare_select_fusion), calls=%async_computation.1 | async-start | bytes 16384 | tf_op jit(solution)/shard_map/all_to_all | solution.py:135
  27.7 5.6 %all-to-all-done.1 = f32[1,8,256]{2,0,1:T(1,128)S(1)} async-done(((f32[1,8,256]{2,0,1:T(1,128)}), f32[1,8,256]{2,0,1:T(1,128)S(1)}, u32[]{:S(2)}, u32[]{:S(2)}) %all-to-all-start.1) | async-done | bytes 8224 | tf_op jit(solution)/shard_map/all_to_all | solution.py:135
  33.4 4.0 %all-to-all-start.2 = ((f32[1,8,256]{2,0,1:T(1,128)}), f32[1,8,256]{2,0,1:T(1,128)S(1)}, u32[]{:S(2)}, u32[]{:S(2)}) async-start(f32[1,8,256]{2,0,1:T(1,128)} %copy.57), calls=%async_computation.2 | async-start | bytes 16384 | tf_op jit(solution)/shard_map/all_to_all | solution.py:134
  37.5 3.1 %all-to-all-done.2 = f32[1,8,256]{2,0,1:T(1,128)S(1)} async-done(((f32[1,8,256]{2,0,1:T(1,128)}), f32[1,8,256]{2,0,1:T(1,128)S(1)}, u32[]{:S(2)}, u32[]{:S(2)}) %all-to-all-start.2) | async-done | bytes 8224 | tf_op jit(solution)/shard_map/all_to_all | solution.py:134
  40.7 12.1 %fusion.31 = bf16[20,1,45,720]{3,2,0,1:T(8,128)(2,1)S(1)} fusion(bf16[20,1,16,720]{3,2,0,1:T(8,128)(2,1)} %collective-permute-done.3, bf16[20,1,45,720]{3,2,0,1:T(8,128)(2,1)S(1)} %bitcast.146, bf16[20,1,16,720]{3,2,0,1:T(8,128)(2,1)} %collective-permute-done.2, f32[]{:T(128)} %bitcast.31, f32[]{:T(128)} %bitcast.30, f32[]{:T(128)} %bitcast.29, ...), kind=kOutput, calls=%fused_computation.44 | convolution fusion | flops 107279912 | bytes 3513668 | tf_op jit(solution)/shard_map/ij,mljk->mlik/dot_general | solution.py:46
  53.7 11.5 %fusion.25 = f32[20,45,5,144]{3,1,2,0:T(8,128)S(1)} fusion(f32[]{:T(128)} %bitcast.58, f32[]{:T(128)} %bitcast.57, f32[]{:T(128)} %bitcast.56, f32[]{:T(128)} %bitcast.55, f32[]{:T(128)} %bitcast.54, f32[]{:T(128)} %bitcast.53, f32[]{:T(128)} %bitcast.52, f32[]{:T(128)} %bitcast.51, f32[]{:T(128)} %bitcast.50, f32[]{:T(128)} %bitcast.49, f32[]{:T(128)} %bitcast.48, ...), kind=kOutput, calls=%fused_computation.38 | convolution fusion | flops 229439232 | bytes 4176772 | tf_op jit(solution)/shard_map/mlibk,kq->mlibq/dot_general | solution.py:59
  65.2 6.4 %copy.55 = f32[20,45,5,144]{3,2,1,0:T(8,128)} copy(f32[20,45,5,144]{3,1,2,0:T(8,128)S(1)} %fusion.25) | data formatting | bytes 5184000 | tf_op jit(solution)/shard_map/mlibk,kq->mlibq/dot_general | solution.py:59
  71.6 4.9 %reshape.136 = f32[20,1,45,720]{3,2,0,1:T(8,128)S(1)} reshape(f32[20,45,5,144]{3,2,1,0:T(8,128)} %copy.55) | data formatting | bytes 5184000 | tf_op jit(solution)/shard_map/reshape | solution.py:60
  76.4 2.4 %multiply_reduce_fusion = f32[45,720]{1,0:T(8,128)} fusion(f32[20,1,45,720]{3,2,0,1:T(8,128)S(1)} %reshape.136, bf16[20,1,45,720]{3,2,1,0:T(8,128)(2,1)} %param.13), kind=kLoop, calls=%fused_computation.22 | loop fusion | flops 1911600 | bytes 4017600 | tf_op jit(solution)/shard_map/reduce_sum | solution.py:129
  78.9 32.7 %all-reduce.4.cloned.1.call-done = f32[720,45]{0,1:T(8,128)} async-done(((f32[720,45]{0,1:T(8,128)}), f32[720,45]{0,1:T(8,128)}) %all-reduce.4.cloned.1.call-update) | async-done | bytes 129616 | tf_op jit(solution)/shard_map/psum | solution.py:145
  111.6 1.1 copy.56
  112.7 3.8 %while.21 = (s32[]{:T(128)}, f32[2,1024]{1,0:T(2,128)S(1)}, s32[2,1024]{1,0:T(2,128)S(1)}, s32[2,1024]{1,0:T(2,128)S(1)}, f32[720,45]{1,0:T(8,128)S(1)}, /*index=5*/s32[]{:T(128)}, s32[]{:T(128)}) while((s32[]{:T(128)}, f32[2,1024]{1,0:T(2,128)S(1)}, s32[2,1024]{1,0:T(2,128)S(1)}, s32[2,1024]{1,0:T(2,128)S(1)}, f32[720,45]{1,0:T(8,128)S(1)}, ...), condition=%wide.region_4.5_spmd, body=%wide.region_2.4_spmd.sunk | while | flops 399005696 | bytes 166549 | solution.py:83
  112.7 1.8 %fusion.179 = f32[1024]{0:T(1024)S(1)} fusion(f32[720,45]{1,0:T(8,128)S(1)} %get-tuple-element.245, s32[1024]{0:T(1024)S(1)} %bitcast.156, s32[1024]{0:T(1024)S(1)} %bitcast.157), kind=kOutput, calls=%fused_computation.4.clone.1 | convolution fusion | flops 399005696 | bytes 141888 | tf_op jit(solution)/shard_map/while/body/eval_jaxpr/dot_general | solution.py:75
  114.6 1.8 %fusion.179 = f32[1024]{0:T(1024)S(1)} fusion(f32[720,45]{1,0:T(8,128)S(1)} %get-tuple-element.245, s32[1024]{0:T(1024)S(1)} %bitcast.156, s32[1024]{0:T(1024)S(1)} %bitcast.157), kind=kOutput, calls=%fused_computation.4.clone.1 | convolution fusion | flops 399005696 | bytes 141888 | tf_op jit(solution)/shard_map/while/body/eval_jaxpr/dot_general | solution.py:75
  116.5 3.1 %while.22 = (s32[]{:T(128)}, f32[45,720]{1,0:T(8,128)S(1)}, s32[2,1024]{1,0:T(2,128)S(1)}, f32[2,1024]{1,0:T(2,128)S(1)}, s32[2,1024]{1,0:T(2,128)S(1)}, /*index=5*/s32[]{:T(128)}, s32[]{:T(128)}) while((s32[]{:T(128)}, f32[45,720]{1,0:T(8,128)S(1)}, s32[2,1024]{1,0:T(2,128)S(1)}, f32[2,1024]{1,0:T(2,128)S(1)}, ...), condition=%wide.region_6.7_spmd.clone, body=%wide.region_5.6_spmd.clone.sunk | while | flops 399025440 | bytes 296159 | solution.py:117
  116.6 1.5 fusion.181
  118.1 1.5 fusion.181
  119.7 3.9 %collective-permute-start.4 = (f32[1,16,720]{2,1,0:T(8,128)S(1)}, f32[1,16,720]{2,1,0:T(8,128)S(1)}, u32[]{:S(2)}, u32[]{:S(2)}) collective-permute-start(f32[1,16,720]{2,1,0:T(8,128)S(1)} %get-tuple-element.119), channel_id=1, source_target_pairs={{0,4},{4,8},{8,12},{12,16},{16,20},{20,24},{24,28},{28,0},{1,5},{5... | collective-permute-start | bytes 138248 | tf_op jit(solution)/shard_map/ppermute | solution.py:14
  123.6 1.2 collective-permute-done.4
  124.7 3.2 %collective-permute-done.5 = f32[1,16,720]{2,1,0:T(8,128)S(1)} collective-permute-done((f32[1,16,720]{2,1,0:T(8,128)S(1)}, f32[1,16,720]{2,1,0:T(8,128)S(1)}, u32[]{:S(2)}, u32[]{:S(2)}) %collective-permute-start.5) | collective-permute-done | bytes 46112 | tf_op jit(solution)/shard_map/ppermute | solution.py:17
  128.0 12.3 %fusion.30 = bf16[20,1,45,720]{3,2,0,1:T(8,128)(2,1)S(1)} fusion(bf16[20,16,720]{2,1,0:T(8,128)(2,1)} %bitcast.8, bf16[20,45,720]{2,1,0:T(8,128)(2,1)S(1)} %bitcast.148, bf16[20,16,720]{2,1,0:T(8,128)(2,1)} %bitcast.5, f32[77,720]{1,0:T(8,128)S(1)} %maximum_bitcast_fusion.6, f32[]{:T(128)} %bitcast.31, f32[]{:T(128)} %bitcast.30, f32[]{:T(128)} %bitcast.29, ...), kind=kOutput, calls=%fused_computation.43 | convolution fusion | flops 109497512 | bytes 3735428 | tf_op jit(solution)/shard_map/ij,mljk->mlik/dot_general | solution.py:46
  141.2 11.5 %fusion.23 = f32[20,45,5,144]{3,1,2,0:T(8,128)S(1)} fusion(f32[]{:T(128)} %bitcast.58, f32[]{:T(128)} %bitcast.57, f32[]{:T(128)} %bitcast.56, f32[]{:T(128)} %bitcast.55, f32[]{:T(128)} %bitcast.54, f32[]{:T(128)} %bitcast.53, f32[]{:T(128)} %bitcast.52, f32[]{:T(128)} %bitcast.51, f32[]{:T(128)} %bitcast.50, f32[]{:T(128)} %bitcast.49, f32[]{:T(128)} %bitcast.48, ...), kind=kOutput, calls=%fused_computation.36 | convolution fusion | flops 229439232 | bytes 4176772 | tf_op jit(solution)/shard_map/mlibk,kq->mlibq/dot_general | solution.py:59
  152.7 6.4 %copy.59 = f32[20,45,5,144]{3,2,1,0:T(8,128)} copy(f32[20,45,5,144]{3,1,2,0:T(8,128)S(1)} %fusion.23) | data formatting | bytes 5184000 | tf_op jit(solution)/shard_map/mlibk,kq->mlibq/dot_general | solution.py:59
  159.1 4.9 %reshape.141 = f32[20,1,45,720]{3,2,0,1:T(8,128)S(1)} reshape(f32[20,45,5,144]{3,2,1,0:T(8,128)} %copy.59) | data formatting | bytes 5184000 | tf_op jit(solution)/shard_map/reshape | solution.py:60
  164.0 1.7 convert_add_fusion
  165.7 4.4 %copy.60 = f32[20,1,45,720]{3,1,2,0:T(1,128)} copy(f32[20,1,45,720]{3,2,0,1:T(8,128)S(1)} %convert_add_fusion) | data formatting | bytes 5184000 | tf_op jit(solution)/shard_map/add | solution.py:153
  (64 shorter events, 5.7 us)
Async XLA Ops:
  6.5 34.1 %copy-start = (bf16[20,1,45,720]{3,2,1,0:T(8,128)(2,1)S(1)}, bf16[20,1,45,720]{3,2,1,0:T(8,128)(2,1)}, u32[]{:S(2)}) copy-start(bf16[20,1,45,720]{3,2,1,0:T(8,128)(2,1)} %param.12) | copy-start | bytes 3888004
  6.5 13.2 %copy-start.7 = (s32[1,8]{1,0:T(1,128)S(1)}, s32[1,8]{1,0:T(1,128)}, u32[]{:S(2)}) copy-start(s32[1,8]{1,0:T(1,128)} %param.19) | copy-start | bytes 100
  6.5 13.2 %copy-start.5 = (f32[1,8,256]{2,1,0:T(8,128)S(1)}, f32[1,8,256]{2,1,0:T(8,128)}, u32[]{:S(2)}) copy-start(f32[1,8,256]{2,1,0:T(8,128)} %param.17) | copy-start | bytes 24580
  6.5 13.9 %copy-start.3 = (bf16[17]{0:T(256)(128)(2,1)S(1)}, bf16[17]{0:T(256)(128)(2,1)}, u32[]{:S(2)}) copy-start(bf16[17]{0:T(256)(128)(2,1)} %param.14) | copy-start | bytes 106
  6.5 14.6 %copy-start.4 = (bf16[17]{0:T(256)(128)(2,1)S(1)}, bf16[17]{0:T(256)(128)(2,1)}, u32[]{:S(2)}) copy-start(bf16[17]{0:T(256)(128)(2,1)} %param.15) | copy-start | bytes 106
  6.5 15.3 %copy-start.6 = (f32[1,8,256]{2,1,0:T(8,128)S(1)}, f32[1,8,256]{2,1,0:T(8,128)}, u32[]{:S(2)}) copy-start(f32[1,8,256]{2,1,0:T(8,128)} %param.16) | copy-start | bytes 24580
  8.1 32.6 %collective-permute-start.2 = (bf16[20,1,16,720]{3,2,0,1:T(8,128)(2,1)S(1)}, bf16[20,1,16,720]{3,2,0,1:T(8,128)(2,1)}, u32[]{:S(2)}, u32[]{:S(2)}) collective-permute-start(bf16[20,1,16,720]{3,2,0,1:T(8,128)(2,1)S(1)} %get-tuple-element.115), channel_id=1, source_target_pairs={{0,4},{4,8},{8,12},{12,16},{16,20},{20,24},{24,28},{28,0},{1,5},{5... | collective-permute-start | bytes 1382408 | tf_op jit(solution)/shard_map/ppermute | solution.py:14
  9.9 30.7 %collective-permute-start.3 = (bf16[20,1,16,720]{3,2,0,1:T(8,128)(2,1)S(1)}, bf16[20,1,16,720]{3,2,0,1:T(8,128)(2,1)}, u32[]{:S(2)}, u32[]{:S(2)}) collective-permute-start(bf16[20,1,16,720]{3,2,0,1:T(8,128)(2,1)S(1)} %get-tuple-element.116), channel_id=1, source_target_pairs={{4,0},{8,4},{12,8},{16,12},{20,16},{24,20},{28,24},{0,28},{5,1},{9... | collective-permute-start | bytes 1382408 | tf_op jit(solution)/shard_map/ppermute | solution.py:17
  11.2 12.0 %all-to-all-start = ((s32[1,8,256]{2,0,1:T(1,128)}), s32[1,8,256]{2,0,1:T(1,128)S(1)}, u32[]{:S(2)}, u32[]{:S(2)}) async-start(s32[1,8,256]{2,0,1:T(1,128)} %copy.48), calls=%async_computation | async-start | bytes 16384 | tf_op jit(solution)/shard_map/all_to_all | solution.py:136
  18.3 109.7 %collective-permute-start = (bf16[20,1,16,720]{3,2,0,1:T(8,128)(2,1)}, bf16[20,1,16,720]{3,2,0,1:T(8,128)(2,1)}, u32[]{:S(2)}, u32[]{:S(2)}) collective-permute-start(bf16[20,1,16,720]{3,2,0,1:T(8,128)(2,1)} %get-tuple-element.117), channel_id=1, source_target_pairs={{0,4},{4,8},{8,12},{12,16},{16,20},{20,24},{24,28},{28,0},{1,5},{5... | collective-permute-start | bytes 1382408 | tf_op jit(solution)/shard_map/ppermute | solution.py:14
  19.8 108.2 %collective-permute-start.1 = (bf16[20,1,16,720]{3,2,0,1:T(8,128)(2,1)S(1)}, bf16[20,1,16,720]{3,2,0,1:T(8,128)(2,1)}, u32[]{:S(2)}, u32[]{:S(2)}) collective-permute-start(bf16[20,1,16,720]{3,2,0,1:T(8,128)(2,1)S(1)} %get-tuple-element.118), channel_id=1, source_target_pairs={{4,0},{8,4},{12,8},{16,12},{20,16},{24,20},{28,24},{0,28},{5,1},{9... | collective-permute-start | bytes 1382408 | tf_op jit(solution)/shard_map/ppermute | solution.py:17
  23.2 10.1 %all-to-all-start.1 = ((f32[1,8,256]{2,0,1:T(1,128)}), f32[1,8,256]{2,0,1:T(1,128)S(1)}, u32[]{:S(2)}, u32[]{:S(2)}) async-start(f32[1,8,256]{2,0,1:T(1,128)} %compare_select_fusion), calls=%async_computation.1 | async-start | bytes 16384 | tf_op jit(solution)/shard_map/all_to_all | solution.py:135
  33.4 7.2 %all-to-all-start.2 = ((f32[1,8,256]{2,0,1:T(1,128)}), f32[1,8,256]{2,0,1:T(1,128)S(1)}, u32[]{:S(2)}, u32[]{:S(2)}) async-start(f32[1,8,256]{2,0,1:T(1,128)} %copy.57), calls=%async_computation.2 | async-start | bytes 16384 | tf_op jit(solution)/shard_map/all_to_all | solution.py:134
  37.3 74.3 %all-reduce.4.cloned.1.call-start = ((), (), s32[]{:S(2)}) async-start(), calls=%async_computation.3 | async-start | bytes 294912 | tf_op jit(solution)/shard_map/psum | solution.py:145
  112.7 3.8 %copy-start.2 = (f32[45,720]{1,0:T(8,128)S(1)}, f32[45,720]{1,0:T(8,128)}, u32[]{:S(2)}) copy-start(f32[45,720]{1,0:T(8,128)} %custom-call) | copy-start | bytes 388804
  116.5 11.5 %copy-start.1 = (bf16[20,1,45,720]{3,2,1,0:T(8,128)(2,1)S(1)}, bf16[20,1,45,720]{3,2,1,0:T(8,128)(2,1)}, u32[]{:S(2)}) copy-start(bf16[20,1,45,720]{3,2,1,0:T(8,128)(2,1)} %param.13) | copy-start | bytes 3888004
  119.7 5.1 %collective-permute-start.4 = (f32[1,16,720]{2,1,0:T(8,128)S(1)}, f32[1,16,720]{2,1,0:T(8,128)S(1)}, u32[]{:S(2)}, u32[]{:S(2)}) collective-permute-start(f32[1,16,720]{2,1,0:T(8,128)S(1)} %get-tuple-element.119), channel_id=1, source_target_pairs={{0,4},{4,8},{8,12},{12,16},{16,20},{20,24},{24,28},{28,0},{1,5},{5... | collective-permute-start | bytes 138248 | tf_op jit(solution)/shard_map/ppermute | solution.py:14
  123.5 4.4 %collective-permute-start.5 = (f32[1,16,720]{2,1,0:T(8,128)S(1)}, f32[1,16,720]{2,1,0:T(8,128)S(1)}, u32[]{:S(2)}, u32[]{:S(2)}) collective-permute-start(f32[1,16,720]{2,1,0:T(8,128)S(1)} %get-tuple-element.120), channel_id=1, source_target_pairs={{4,0},{8,4},{12,8},{16,12},{20,16},{24,20},{28,24},{0,28},{5,1},{9... | collective-permute-start | bytes 138248 | tf_op jit(solution)/shard_map/ppermute | solution.py:17
Sparse Core Ops, SparseCore 0:
  79.0 32.5 all-reduce.3
where the time goes:
time: 178 us; the launch traced here: 177 us
  matrix products  54 us (30%)
  waiting for transfers between devices  46.7 us (26%)
  local copies, waits for them, and re-layouts  37 us (21%)
  starting transfers between devices  20.5 us (12%)
  between operations  13.7 us (8%)
  other arithmetic  4.93 us (3%)
    psum x1, waiting for transfers between devices, local(): increment = lax.psum(member_sum, 'mem')  32.7 us
    dot_general x2, matrix products, localize(): jnp.einsum('ij,mljk->mlik', band_lon, extended, preferred_element_type=jn...  24.4 us
    dot_general x2, matrix products, localize(): jnp.einsum('mlibk,kq->mlibq', windows, band_blocks, preferred_element_typ...  23 us
    dot_general x2, local copies, waits for them, and re-layouts, localize(): jnp.einsum('mlibk,kq->mlibq', windows, band_blocks, preferred_element_typ...  12.8 us
    reshape x2, local copies, waits for them, and re-layouts, localize(): return result.reshape(members_here, levels, lon_cells, lat_cells)  9.75 us
    ppermute x3, starting transfers between devices, extended_2(): lax.ppermute(lax.slice_in_dim(block, block.shape[dim] - width, None, axis...  7.17 us
    all_to_all x1, waiting for transfers between devices, local(): lax.all_to_all(weights, 'tile', split_axis=1, concat_axis=0, tiled=True)  5.65 us
    all_to_all x1, starting transfers between devices, local(): lax.all_to_all(cell_index, 'tile', split_axis=1, concat_axis=0, tiled=True)  4.92 us
  transfers between devices with their start and end apart: 10, of which 6 were waited for; matrix products, arithmetic and copies ran while one was open for 30% of the time, Pallas kernels for 0%

commit v1 on v0

--- a/solution.py
+++ b/solution.py
@@ -3,6 +3,41 @@
 import jax.numpy as jnp
 from jax import lax
 from jax.sharding import PartitionSpec as P
+
+
+def extend_types(mine, along_dim, matrix):
+    outcome_arr = mine.shape
+    w_next = mine.reshape(
+        *outcome_arr[:along_dim],
+        matrix,
+        outcome_arr[along_dim] // matrix,
+        *outcome_arr[along_dim + 1 :]
+    )
+    return jnp.moveaxis(w_next, along_dim, 0)
+
+
+def connect_pieces_all(block_in, where_dim):
+    block_in = jnp.moveaxis(block_in, 0, where_dim)
+    tmp = block_in.shape
+    return block_in.reshape(
+        *tmp[:where_dim], tmp[where_dim] * tmp[where_dim + 1], *tmp[where_dim + 2 :]
+    )
+
+
+def resolve_chunk(row_data, device_axis, buf, array_here):
+    mid_arr = lax.axis_size(device_axis)
+    view_out, part_next = (mid_arr, lax.axis_index(device_axis))
+    frame_out = extend_types(row_data, buf, view_out)
+    outer = frame_out
+    for j in range(1, view_out):
+        n_now, met_up = ((part_next + j) % view_out, (part_next - j) % view_out)
+        current_block = lax.dynamic_index_in_dim(frame_out, n_now, 0)
+        all_blocks = []
+        for k0 in range(view_out):
+            all_blocks.append((k0, (k0 + j) % view_out))
+        reply = lax.ppermute(current_block, device_axis, all_blocks)
+        outer = lax.dynamic_update_slice_in_dim(outer, reply, met_up, axis=0)
+    return connect_pieces_all(outer, array_here)
 
 
 def extended_2(block, sides, width):
@@ -133,7 +168,7 @@
     received = (
         lax.all_to_all(innov, "tile", split_axis=1, concat_axis=0, tiled=True),
         lax.all_to_all(weights, "tile", split_axis=1, concat_axis=0, tiled=True),
-        lax.all_to_all(cell_index, "tile", split_axis=1, concat_axis=0, tiled=True),
+        resolve_chunk(cell_index, "tile", 1, 0),
     )
     observed = received[0].reshape(-1)
     weight_recv = received[1].reshape(-1)

time: 178 us -> 171 us (0.961)
  waiting for transfers between devices: 46.7 us -> 33.6 us
  starting transfers between devices: 20.5 us -> 23.4 us
  local copies, waits for them, and re-layouts: 37 us -> 39.2 us
    psum x1, waiting for transfers between devices: 32.7 us -> 24.9 us  [local(): increment = lax.psum(member_sum, 'mem')]
    all_to_all x1, waiting for transfers between devices: 5.65 us -> 0.01 us  [local(): lax.all_to_all(weights, 'tile', split_axis=1, concat_axis=0, tiled=True)]
    ppermute x0 -> x7, starting transfers between devices: none -> 5.03 us  [resolve_chunk(): reply = lax.ppermute(current_block, device_axis, all_blocks)]
    all_to_all x1 -> x0, starting transfers between devices: 4.92 us -> none  [local(): lax.all_to_all(cell_index, 'tile', split_axis=1, concat_axis=0, tiled=True)]
    slice x2, local copies, waits for them, and re-layouts: 1.41 us -> 3.97 us  [band_from(): band = band + jnp.where(offsets == offset, taps[offset], 0.0)]
  transfers between devices with their start and end apart: 10 -> 16, of which waited for: 6 -> 6; matrix products, arithmetic and copies ran while one was open for 30% -> 32% of each run, Pallas kernels for 0% -> 0%
where the time goes in v1:
time: 171 us; the launch traced here: 170 us
  matrix products  54.3 us (32%)
  local copies, waits for them, and re-layouts  39.2 us (23%)
  waiting for transfers between devices  33.6 us (20%)
  starting transfers between devices  23.4 us (14%)
  between operations  13.7 us (8%)
  other arithmetic  5.54 us (3%)
    dot_general x2, matrix products, localize(): jnp.einsum('ij,mljk->mlik', band_lon, extended, preferred_element_type=jn...  25.2 us
    psum x1, waiting for transfers between devices, local(): increment = lax.psum(member_sum, 'mem')  24.9 us
    dot_general x2, matrix products, localize(): jnp.einsum('mlibk,kq->mlibq', windows, band_blocks, preferred_element_typ...  22.5 us
    dot_general x2, local copies, waits for them, and re-layouts, localize(): jnp.einsum('mlibk,kq->mlibq', windows, band_blocks, preferred_element_typ...  12.8 us
    reshape x2, local copies, waits for them, and re-layouts, localize(): return result.reshape(members_here, levels, lon_cells, lat_cells)  9.75 us
    ppermute x3, starting transfers between devices, extended_2(): lax.ppermute(lax.slice_in_dim(block, block.shape[dim] - width, None, axis...  8.32 us
    all_to_all x1, starting transfers between devices, local(): lax.all_to_all(innov, 'tile', split_axis=1, concat_axis=0, tiled=True)  5.05 us
    ppermute x7, starting transfers between devices, resolve_chunk(): reply = lax.ppermute(current_block, device_axis, all_blocks)  5.03 us
  transfers between devices with their start and end apart: 16, of which 6 were waited for; matrix products, arithmetic and copies ran while one was open for 32% of the time, Pallas kernels for 0%

profile of v1, /device:TPU:11, one launch (start us, length us, event | category | flops | bytes accessed | tf_op | source)
XLA Modules:
  0.0 169.9 jit_solution(9055866673311708937)
XLA Ops:
  7.4 1.4 fusion.173
  9.5 2.0 %collective-permute-start.9 = (bf16[20,1,16,720]{3,2,0,1:T(8,128)(2,1)S(1)}, bf16[20,1,16,720]{3,2,0,1:T(8,128)(2,1)}, u32[]{:S(2)}, u32[]{:S(2)}) collective-permute-start(bf16[20,1,16,720]{3,2,0,1:T(8,128)(2,1)S(1)} %get-tuple-element.113), channel_id=1, source_target_pairs={{0,4},{4,8},{8,12},{12,16},{16,20},{20,24},{24,28},{28,0},{1,5},{5... | collective-permute-start | bytes 1382408 | tf_op jit(solution)/shard_map/ppermute | solution.py:49
  13.2 1.4 compare_select_fusion
  14.5 4.2 %all-to-all-start = ((f32[1,8,256]{2,0,1:T(1,128)}), f32[1,8,256]{2,0,1:T(1,128)S(1)}, u32[]{:S(2)}, u32[]{:S(2)}) async-start(f32[1,8,256]{2,0,1:T(1,128)} %compare_select_fusion), calls=%async_computation | async-start | bytes 16384 | tf_op jit(solution)/shard_map/all_to_all | solution.py:170
  18.7 2.0 %fusion.177 = (f32[1]{0:T(128)}, f32[1]{0:T(128)}, f32[1]{0:T(128)}, f32[1]{0:T(128)}, f32[1]{0:T(128)}, /*index=5*/f32[1]{0:T(128)}, f32[1]{0:T(128)}, f32[1]{0...) fusion(bf16[17]{0:T(256)(128)(2,1)} %param.14), kind=kLoop, calls=%fused_computation.217 | loop fusion | bytes 136 | tf_op jit(solution)/shard_map/slice | solution.py:62
  20.7 2.0 %fusion.176 = (f32[1]{0:T(128)}, f32[1]{0:T(128)}, f32[1]{0:T(128)}, f32[1]{0:T(128)}, f32[1]{0:T(128)}, /*index=5*/f32[1]{0:T(128)}, f32[1]{0:T(128)}, f32[1]{0...) fusion(bf16[17]{0:T(256)(128)(2,1)} %param.15), kind=kLoop, calls=%fused_computation.216 | loop fusion | bytes 136 | tf_op jit(solution)/shard_map/slice | solution.py:62
  22.7 2.2 %fusion.174 = (bf16[20,1,16,720]{3,2,0,1:T(8,128)(2,1)}, bf16[20,1,16,720]{3,2,0,1:T(8,128)(2,1)S(1)}) fusion(bf16[20,1,45,720]{3,2,0,1:T(8,128)(2,1)} %bitcast.174), kind=kLoop, calls=%fused_computation.214 | loop fusion | bytes 1843200 | tf_op jit(solution)/shard_map/slice | solution.py:50
  24.9 1.2 collective-permute-start.5
  29.1 2.5 %collective-permute-start = (bf16[20,1,16,720]{3,2,0,1:T(8,128)(2,1)}, bf16[20,1,16,720]{3,2,0,1:T(8,128)(2,1)}, u32[]{:S(2)}, u32[]{:S(2)}) collective-permute-start(bf16[20,1,16,720]{3,2,0,1:T(8,128)(2,1)} %get-tuple-element.115), channel_id=1, source_target_pairs={{0,4},{4,8},{8,12},{12,16},{16,20},{20,24},{24,28},{28,0},{1,5},{5... | collective-permute-start | bytes 1382408 | tf_op jit(solution)/shard_map/ppermute | solution.py:49
  32.7 12.5 %fusion.31 = bf16[20,1,45,720]{3,2,0,1:T(8,128)(2,1)S(1)} fusion(bf16[20,1,16,720]{3,2,0,1:T(8,128)(2,1)} %collective-permute-done.10, bf16[20,1,45,720]{3,2,0,1:T(8,128)(2,1)S(1)} %bitcast.173, bf16[20,1,16,720]{3,2,0,1:T(8,128)(2,1)} %collective-permute-done.9, f32[]{:T(128)} %bitcast.39, f32[]{:T(128)} %bitcast.38, f32[]{:T(128)} %bitcast.37, ...), kind=kOutput, calls=%fused_computation.44 | convolution fusion | flops 107279912 | bytes 3513668 | tf_op jit(solution)/shard_map/ij,mljk->mlik/dot_general | solution.py:81
  46.1 11.3 %fusion.25 = f32[20,45,5,144]{3,1,2,0:T(8,128)S(1)} fusion(f32[]{:T(128)} %bitcast.66, f32[]{:T(128)} %bitcast.65, f32[]{:T(128)} %bitcast.64, f32[]{:T(128)} %bitcast.63, f32[]{:T(128)} %bitcast.62, f32[]{:T(128)} %bitcast.61, f32[]{:T(128)} %bitcast.60, f32[]{:T(128)} %bitcast.59, f32[]{:T(128)} %bitcast.58, f32[]{:T(128)} %bitcast.57, f32[]{:T(128)} %bitcast.56, ...), kind=kOutput, calls=%fused_computation.38 | convolution fusion | flops 229439232 | bytes 4176772 | tf_op jit(solution)/shard_map/mlibk,kq->mlibq/dot_general | solution.py:94
  57.4 6.4 %copy.53 = f32[20,45,5,144]{3,2,1,0:T(8,128)} copy(f32[20,45,5,144]{3,1,2,0:T(8,128)S(1)} %fusion.25) | data formatting | bytes 5184000 | tf_op jit(solution)/shard_map/mlibk,kq->mlibq/dot_general | solution.py:94
  63.8 4.9 %reshape.138 = f32[20,1,45,720]{3,2,0,1:T(8,128)S(1)} reshape(f32[20,45,5,144]{3,2,1,0:T(8,128)} %copy.53) | data formatting | bytes 5184000 | tf_op jit(solution)/shard_map/reshape | solution.py:95
  68.7 2.4 %multiply_reduce_fusion = f32[45,720]{1,0:T(8,128)} fusion(f32[20,1,45,720]{3,2,0,1:T(8,128)S(1)} %reshape.138, bf16[20,1,45,720]{3,2,1,0:T(8,128)(2,1)} %param.13), kind=kLoop, calls=%fused_computation.22 | loop fusion | flops 1911600 | bytes 4017600 | tf_op jit(solution)/shard_map/reduce_sum | solution.py:164
  71.1 5.1 %all-to-all-start.1 = ((f32[1,8,256]{2,0,1:T(1,128)}), f32[1,8,256]{2,0,1:T(1,128)S(1)}, u32[]{:S(2)}, u32[]{:S(2)}) async-start(f32[1,8,256]{2,0,1:T(1,128)} %copy.55), calls=%async_computation.1 | async-start | bytes 16384 | tf_op jit(solution)/shard_map/all_to_all | solution.py:169
  76.2 3.3 %all-to-all-done.1 = f32[1,8,256]{2,0,1:T(1,128)S(1)} async-done(((f32[1,8,256]{2,0,1:T(1,128)}), f32[1,8,256]{2,0,1:T(1,128)S(1)}, u32[]{:S(2)}, u32[]{:S(2)}) %all-to-all-start.1) | async-done | bytes 8224 | tf_op jit(solution)/shard_map/all_to_all | solution.py:169
  79.5 24.9 %all-reduce.4.cloned.1.call-done = f32[720,45]{0,1:T(8,128)} async-done(((f32[720,45]{0,1:T(8,128)}), f32[720,45]{0,1:T(8,128)}) %all-reduce.4.cloned.1.call-update) | async-done | bytes 129616 | tf_op jit(solution)/shard_map/psum | solution.py:180
  105.6 3.8 %while.21 = (s32[]{:T(128)}, f32[2,1024]{1,0:T(2,128)S(1)}, s32[2,1024]{1,0:T(2,128)S(1)}, s32[2,1024]{1,0:T(2,128)S(1)}, f32[720,45]{1,0:T(8,128)S(1)}, /*index=5*/s32[]{:T(128)}, s32[]{:T(128)}) while((s32[]{:T(128)}, f32[2,1024]{1,0:T(2,128)S(1)}, s32[2,1024]{1,0:T(2,128)S(1)}, s32[2,1024]{1,0:T(2,128)S(1)}, f32[720,45]{1,0:T(8,128)S(1)}, ...), condition=%wide.region_4.5_spmd, body=%wide.region_2.4_spmd.sunk | while | flops 399005696 | bytes 166549 | solution.py:118
  105.6 1.8 %fusion.186 = f32[1024]{0:T(1024)S(1)} fusion(f32[720,45]{1,0:T(8,128)S(1)} %get-tuple-element.252, s32[1024]{0:T(1024)S(1)} %bitcast.184, s32[1024]{0:T(1024)S(1)} %bitcast.185), kind=kOutput, calls=%fused_computation.4.clone.1 | convolution fusion | flops 399005696 | bytes 141888 | tf_op jit(solution)/shard_map/while/body/eval_jaxpr/dot_general | solution.py:110
  107.5 1.8 %fusion.186 = f32[1024]{0:T(1024)S(1)} fusion(f32[720,45]{1,0:T(8,128)S(1)} %get-tuple-element.252, s32[1024]{0:T(1024)S(1)} %bitcast.184, s32[1024]{0:T(1024)S(1)} %bitcast.185), kind=kOutput, calls=%fused_computation.4.clone.1 | convolution fusion | flops 399005696 | bytes 141888 | tf_op jit(solution)/shard_map/while/body/eval_jaxpr/dot_general | solution.py:110
  109.4 3.1 %while.22 = (s32[]{:T(128)}, f32[45,720]{1,0:T(8,128)S(1)}, s32[2,1024]{1,0:T(2,128)S(1)}, f32[2,1024]{1,0:T(2,128)S(1)}, s32[2,1024]{1,0:T(2,128)S(1)}, /*index=5*/s32[]{:T(128)}, s32[]{:T(128)}) while((s32[]{:T(128)}, f32[45,720]{1,0:T(8,128)S(1)}, s32[2,1024]{1,0:T(2,128)S(1)}, f32[2,1024]{1,0:T(2,128)S(1)}, ...), condition=%wide.region_6.7_spmd.clone, body=%wide.region_5.6_spmd.clone.sunk | while | flops 399025440 | bytes 296159 | solution.py:152
  109.5 1.5 fusion.188
  111.0 1.5 fusion.188
  112.5 3.9 %collective-permute-start.11 = (f32[1,16,720]{2,1,0:T(8,128)S(1)}, f32[1,16,720]{2,1,0:T(8,128)S(1)}, u32[]{:S(2)}, u32[]{:S(2)}) collective-permute-start(f32[1,16,720]{2,1,0:T(8,128)S(1)} %get-tuple-element.117), channel_id=1, source_target_pairs={{0,4},{4,8},{8,12},{12,16},{16,20},{20,24},{24,28},{28,0},{1,5},{5... | collective-permute-start | bytes 138248 | tf_op jit(solution)/shard_map/ppermute | solution.py:49
  116.4 1.2 collective-permute-done.11
  117.6 3.2 %collective-permute-done.12 = f32[1,16,720]{2,1,0:T(8,128)S(1)} collective-permute-done((f32[1,16,720]{2,1,0:T(8,128)S(1)}, f32[1,16,720]{2,1,0:T(8,128)S(1)}, u32[]{:S(2)}, u32[]{:S(2)}) %collective-permute-start.12) | collective-permute-done | bytes 46112 | tf_op jit(solution)/shard_map/ppermute | solution.py:52
  120.9 12.7 %fusion.30 = bf16[20,1,45,720]{3,2,0,1:T(8,128)(2,1)S(1)} fusion(bf16[20,16,720]{2,1,0:T(8,128)(2,1)} %bitcast.8, bf16[20,45,720]{2,1,0:T(8,128)(2,1)S(1)} %bitcast.175, bf16[20,16,720]{2,1,0:T(8,128)(2,1)} %bitcast.5, f32[77,720]{1,0:T(8,128)S(1)} %maximum_bitcast_fusion.6, f32[]{:T(128)} %bitcast.39, f32[]{:T(128)} %bitcast.38, f32[]{:T(128)} %bitcast.37, ...), kind=kOutput, calls=%fused_computation.43 | convolution fusion | flops 109497512 | bytes 3735428 | tf_op jit(solution)/shard_map/ij,mljk->mlik/dot_general | solution.py:81
  134.5 11.3 %fusion.23 = f32[20,45,5,144]{3,1,2,0:T(8,128)S(1)} fusion(f32[]{:T(128)} %bitcast.66, f32[]{:T(128)} %bitcast.65, f32[]{:T(128)} %bitcast.64, f32[]{:T(128)} %bitcast.63, f32[]{:T(128)} %bitcast.62, f32[]{:T(128)} %bitcast.61, f32[]{:T(128)} %bitcast.60, f32[]{:T(128)} %bitcast.59, f32[]{:T(128)} %bitcast.58, f32[]{:T(128)} %bitcast.57, f32[]{:T(128)} %bitcast.56, ...), kind=kOutput, calls=%fused_computation.36 | convolution fusion | flops 229439232 | bytes 4176772 | tf_op jit(solution)/shard_map/mlibk,kq->mlibq/dot_general | solution.py:94
  145.8 6.4 %copy.57 = f32[20,45,5,144]{3,2,1,0:T(8,128)} copy(f32[20,45,5,144]{3,1,2,0:T(8,128)S(1)} %fusion.23) | data formatting | bytes 5184000 | tf_op jit(solution)/shard_map/mlibk,kq->mlibq/dot_general | solution.py:94
  152.2 4.9 %reshape.143 = f32[20,1,45,720]{3,2,0,1:T(8,128)S(1)} reshape(f32[20,45,5,144]{3,2,1,0:T(8,128)} %copy.57) | data formatting | bytes 5184000 | tf_op jit(solution)/shard_map/reshape | solution.py:95
  157.0 1.7 convert_add_fusion
  158.7 4.4 %copy.58 = f32[20,1,45,720]{3,1,2,0:T(1,128)} copy(f32[20,1,45,720]{3,2,0,1:T(8,128)S(1)} %convert_add_fusion) | data formatting | bytes 5184000 | tf_op jit(solution)/shard_map/add | solution.py:188
  (76 shorter events, 10.5 us)
Async XLA Ops:
  6.5 26.2 %copy-start = (bf16[20,1,45,720]{3,2,1,0:T(8,128)(2,1)S(1)}, bf16[20,1,45,720]{3,2,1,0:T(8,128)(2,1)}, u32[]{:S(2)}) copy-start(bf16[20,1,45,720]{3,2,1,0:T(8,128)(2,1)} %param.12) | copy-start | bytes 3888004
  6.5 21.6 %copy-start.3 = (f32[1,8,256]{2,1,0:T(8,128)S(1)}, f32[1,8,256]{2,1,0:T(8,128)}, u32[]{:S(2)}) copy-start(f32[1,8,256]{2,1,0:T(8,128)} %param.16) | copy-start | bytes 24580
  8.8 24.0 %collective-permute-start.10 = (bf16[20,1,16,720]{3,2,0,1:T(8,128)(2,1)S(1)}, bf16[20,1,16,720]{3,2,0,1:T(8,128)(2,1)}, u32[]{:S(2)}, u32[]{:S(2)}) collective-permute-start(bf16[20,1,16,720]{3,2,0,1:T(8,128)(2,1)S(1)} %get-tuple-element.114), channel_id=1, source_target_pairs={{4,0},{8,4},{12,8},{16,12},{20,16},{24,20},{28,24},{0,28},{5,1},{9... | collective-permute-start | bytes 1382408 | tf_op jit(solution)/shard_map/ppermute | solution.py:52
  9.5 23.2 %collective-permute-start.9 = (bf16[20,1,16,720]{3,2,0,1:T(8,128)(2,1)S(1)}, bf16[20,1,16,720]{3,2,0,1:T(8,128)(2,1)}, u32[]{:S(2)}, u32[]{:S(2)}) collective-permute-start(bf16[20,1,16,720]{3,2,0,1:T(8,128)(2,1)S(1)} %get-tuple-element.113), channel_id=1, source_target_pairs={{0,4},{4,8},{8,12},{12,16},{16,20},{20,24},{24,28},{28,0},{1,5},{5... | collective-permute-start | bytes 1382408 | tf_op jit(solution)/shard_map/ppermute | solution.py:49
  11.5 13.4 %collective-permute-start.2 = (s32[1,1,1,256]{3,0,2,1:T(1,128)S(1)}, s32[1,1,1,256]{3,0,2,1:T(1,128)S(1)}, u32[]{:S(2)}, u32[]{:S(2)}) collective-permute-start(s32[1,1,1,256]{3,0,2,1:T(1,128)S(1)} %get-tuple-element.128), channel_id=1, source_target_pairs={{0,4},{4,8},{8,12},{12,16},{16,20},{20,24},{24,28},{28,0},{1,5},{5... | collective-permute-start | bytes 3080 | tf_op jit(solution)/shard_map/ppermute | solution.py:38
  11.5 14.6 %collective-permute-start.3 = (s32[1,1,1,256]{3,0,2,1:T(1,128)S(1)}, s32[1,1,1,256]{3,0,2,1:T(1,128)S(1)}, u32[]{:S(2)}, u32[]{:S(2)}) collective-permute-start(s32[1,1,1,256]{3,0,2,1:T(1,128)S(1)} %get-tuple-element.127), channel_id=1, source_target_pairs={{0,8},{4,12},{8,16},{12,20},{16,24},{20,28},{24,0},{28,4},{1,9},{5... | collective-permute-start | bytes 3080 | tf_op jit(solution)/shard_map/ppermute | solution.py:38
  12.4 14.6 %collective-permute-start.4 = (s32[1,1,1,256]{3,0,2,1:T(1,128)S(1)}, s32[1,1,1,256]{3,0,2,1:T(1,128)S(1)}, u32[]{:S(2)}, u32[]{:S(2)}) collective-permute-start(s32[1,1,1,256]{3,0,2,1:T(1,128)S(1)} %get-tuple-element.126), channel_id=1, source_target_pairs={{0,12},{4,16},{8,20},{12,24},{16,28},{20,0},{24,4},{28,8},{1,13},{... | collective-permute-start | bytes 3080 | tf_op jit(solution)/shard_map/ppermute | solution.py:38
  14.5 56.5 %all-to-all-start = ((f32[1,8,256]{2,0,1:T(1,128)}), f32[1,8,256]{2,0,1:T(1,128)S(1)}, u32[]{:S(2)}, u32[]{:S(2)}) async-start(f32[1,8,256]{2,0,1:T(1,128)} %compare_select_fusion), calls=%async_computation | async-start | bytes 16384 | tf_op jit(solution)/shard_map/all_to_all | solution.py:170
  18.7 85.7 %all-reduce.4.cloned.1.call-start = ((), (), s32[]{:S(2)}) async-start(), calls=%async_computation.2 | async-start | bytes 294912 | tf_op jit(solution)/shard_map/psum | solution.py:180
  24.9 3.8 %collective-permute-start.5 = (s32[1,1,1,256]{3,0,2,1:T(1,128)S(1)}, s32[1,1,1,256]{3,0,2,1:T(1,128)S(1)}, u32[]{:S(2)}, u32[]{:S(2)}) collective-permute-start(s32[1,1,1,256]{3,0,2,1:T(1,128)S(1)} %get-tuple-element.125), channel_id=1, source_target_pairs={{0,16},{4,20},{8,24},{12,28},{16,0},{20,4},{24,8},{28,12},{1,17},{... | collective-permute-start | bytes 3080 | tf_op jit(solution)/shard_map/ppermute | solution.py:38
  26.1 3.0 %collective-permute-start.6 = (s32[1,1,1,256]{3,0,2,1:T(1,128)S(1)}, s32[1,1,1,256]{3,0,2,1:T(1,128)S(1)}, u32[]{:S(2)}, u32[]{:S(2)}) collective-permute-start(s32[1,1,1,256]{3,0,2,1:T(1,128)S(1)} %get-tuple-element.124), channel_id=1, source_target_pairs={{0,20},{4,24},{8,28},{12,0},{16,4},{20,8},{24,12},{28,16},{1,21},{... | collective-permute-start | bytes 3080 | tf_op jit(solution)/shard_map/ppermute | solution.py:38
  26.9 4.7 %collective-permute-start.7 = (s32[1,1,1,256]{3,0,2,1:T(1,128)S(1)}, s32[1,1,1,256]{3,0,2,1:T(1,128)S(1)}, u32[]{:S(2)}, u32[]{:S(2)}) collective-permute-start(s32[1,1,1,256]{3,0,2,1:T(1,128)S(1)} %get-tuple-element.129), channel_id=1, source_target_pairs={{0,24},{4,28},{8,0},{12,4},{16,8},{20,12},{24,16},{28,20},{1,25},{... | collective-permute-start | bytes 3080 | tf_op jit(solution)/shard_map/ppermute | solution.py:38
  28.7 3.9 %collective-permute-start.8 = (s32[1,1,1,256]{3,0,2,1:T(1,128)S(1)}, s32[1,1,1,256]{3,0,2,1:T(1,128)S(1)}, u32[]{:S(2)}, u32[]{:S(2)}) collective-permute-start(s32[1,1,1,256]{3,0,2,1:T(1,128)S(1)} %get-tuple-element.123), channel_id=1, source_target_pairs={{0,28},{4,0},{8,4},{12,8},{16,12},{20,16},{24,20},{28,24},{1,29},{... | collective-permute-start | bytes 3080 | tf_op jit(solution)/shard_map/ppermute | solution.py:38
  29.1 91.8 %collective-permute-start = (bf16[20,1,16,720]{3,2,0,1:T(8,128)(2,1)}, bf16[20,1,16,720]{3,2,0,1:T(8,128)(2,1)}, u32[]{:S(2)}, u32[]{:S(2)}) collective-permute-start(bf16[20,1,16,720]{3,2,0,1:T(8,128)(2,1)} %get-tuple-element.115), channel_id=1, source_target_pairs={{0,4},{4,8},{8,12},{12,16},{16,20},{20,24},{24,28},{28,0},{1,5},{5... | collective-permute-start | bytes 1382408 | tf_op jit(solution)/shard_map/ppermute | solution.py:49
  31.6 89.3 %collective-permute-start.1 = (bf16[20,1,16,720]{3,2,0,1:T(8,128)(2,1)S(1)}, bf16[20,1,16,720]{3,2,0,1:T(8,128)(2,1)}, u32[]{:S(2)}, u32[]{:S(2)}) collective-permute-start(bf16[20,1,16,720]{3,2,0,1:T(8,128)(2,1)S(1)} %get-tuple-element.116), channel_id=1, source_target_pairs={{4,0},{8,4},{12,8},{16,12},{20,16},{24,20},{28,24},{0,28},{5,1},{9... | collective-permute-start | bytes 1382408 | tf_op jit(solution)/shard_map/ppermute | solution.py:52
  71.1 8.4 %all-to-all-start.1 = ((f32[1,8,256]{2,0,1:T(1,128)}), f32[1,8,256]{2,0,1:T(1,128)S(1)}, u32[]{:S(2)}, u32[]{:S(2)}) async-start(f32[1,8,256]{2,0,1:T(1,128)} %copy.55), calls=%async_computation.1 | async-start | bytes 16384 | tf_op jit(solution)/shard_map/all_to_all | solution.py:169
  105.6 3.8 %copy-start.2 = (f32[45,720]{1,0:T(8,128)S(1)}, f32[45,720]{1,0:T(8,128)}, u32[]{:S(2)}) copy-start(f32[45,720]{1,0:T(8,128)} %custom-call) | copy-start | bytes 388804
  109.4 11.5 %copy-start.1 = (bf16[20,1,45,720]{3,2,1,0:T(8,128)(2,1)S(1)}, bf16[20,1,45,720]{3,2,1,0:T(8,128)(2,1)}, u32[]{:S(2)}) copy-start(bf16[20,1,45,720]{3,2,1,0:T(8,128)(2,1)} %param.13) | copy-start | bytes 3888004
  112.5 5.1 %collective-permute-start.11 = (f32[1,16,720]{2,1,0:T(8,128)S(1)}, f32[1,16,720]{2,1,0:T(8,128)S(1)}, u32[]{:S(2)}, u32[]{:S(2)}) collective-permute-start(f32[1,16,720]{2,1,0:T(8,128)S(1)} %get-tuple-element.117), channel_id=1, source_target_pairs={{0,4},{4,8},{8,12},{12,16},{16,20},{20,24},{24,28},{28,0},{1,5},{5... | collective-permute-start | bytes 138248 | tf_op jit(solution)/shard_map/ppermute | solution.py:49
  116.4 4.4 %collective-permute-start.12 = (f32[1,16,720]{2,1,0:T(8,128)S(1)}, f32[1,16,720]{2,1,0:T(8,128)S(1)}, u32[]{:S(2)}, u32[]{:S(2)}) collective-permute-start(f32[1,16,720]{2,1,0:T(8,128)S(1)} %get-tuple-element.118), channel_id=1, source_target_pairs={{4,0},{8,4},{12,8},{16,12},{20,16},{24,20},{28,24},{0,28},{5,1},{9... | collective-permute-start | bytes 138248 | tf_op jit(solution)/shard_map/ppermute | solution.py:52
Sparse Core Ops, SparseCore 0:
  71.2 33.2 all-reduce.3
